TPU v7x, 32 devices: a whole 2x2x4 slice. The times are simulated.
32 devices in a mesh: groups: 2 (over x), chan: 16 (over z, y, core).
Axes of the slice: x: 2, y: 2, z: 4, core: 2. Of those that a mesh axis runs over, the one named last changes fastest.
Arguments:
- traces: float32 [2048, 1152], P(('groups', 'chan')), parts along dimension 0, as said below
- good_mask: int32 [2048], P(('groups', 'chan')), parts along dimension 0, may hold values 0 or 1
Outputs:
- correlations: bfloat16 [2048, 64, 1024], P(('groups', 'chan')), parts along dimension 0
There are 2 independent parts, one for each index of `groups`. A program takes and returns all parts, laid end to end along the dimension named above; each array names one. Nothing has to cross between parts.
Inputs may be any that keep to these rules, and one draw needn't show every extreme that they name: `traces`: traces of order one.
All inputs are finite; a program needn't handle non-finite values. No bound on the sum of `good_mask` on one device may be relied on, other than what follows from the above.
Results may differ from a plain program's by a relative error of at most 0.0053.
Values may be sent and summed in bfloat16 or wider, within the bound.
No kernel may reach another device: no remote copies, remote signals or barrier semaphores. Data moves between devices by JAX's collectives and lax.ppermute only.
A program may use at most 128 MiB of HBM per device.

v0:
```python
import math
import jax
import jax.numpy as jnp
from jax import lax
from jax.sharding import PartitionSpec as P

NW = 256
NF = 128
HOP = 128
LAGS = 64
NWIN = 8


def forward_table(width, bins):
    samples = jnp.arange(width)
    freqs = jnp.arange(1, bins + 1)
    phase = samples[:, None] * freqs[None, :] % width
    theta = 2.0 * math.pi * phase.astype(jnp.float32) / width
    hann = 0.5 - 0.5 * jnp.cos(2.0 * math.pi * samples.astype(jnp.float32) / width)
    return jnp.concatenate(
        [hann[:, None] * jnp.cos(theta), -hann[:, None] * jnp.sin(theta)], axis=1
    )


def lag_rotation(width, bins, lag_count):
    freqs = jnp.arange(1, bins + 1)
    lags = jnp.arange(lag_count) - lag_count // 2
    phase = freqs[:, None] * lags[None, :] % width
    theta = 2.0 * math.pi * phase.astype(jnp.float32) / width
    return (jnp.cos(theta), jnp.sin(theta))


def whiten(traces, good_mask):
    channels_here = traces.shape[0]
    good = good_mask.astype(jnp.float32)
    total, count = lax.psum((jnp.sum(traces * good[:, None], axis=0), jnp.sum(good)), "chan")
    common = total / jnp.maximum(count, 1.0)
    clean = (traces - common[None, :]) * good[:, None]
    halves = clean.reshape(channels_here, NWIN + 1, HOP)
    segments = jnp.concatenate([halves[:, :-1], halves[:, 1:]], axis=2)
    spectrum = jnp.einsum(
        "cwn,nk->wck", segments, forward_table(NW, NF), precision=lax.Precision.HIGHEST
    )
    real_part = spectrum[..., :NF]
    imag_part = spectrum[..., NF:]
    power = real_part * real_part + imag_part * imag_part
    magnitude = jnp.sqrt(power)
    level = jnp.sqrt(jnp.mean(power, axis=-1, keepdims=True) + 1e-06)
    denom = jnp.maximum(magnitude, 0.3 * level)
    return jnp.concatenate([real_part / denom, imag_part / denom], axis=-1).astype(jnp.bfloat16)


def shards(traces, good_mask):
    whitened = whiten(traces, good_mask)
    others = lax.all_gather(whitened, "chan", axis=1, tiled=True)
    own = whitened.astype(jnp.float32)
    own_real, own_imag = (own[..., :NF], own[..., NF:])
    cos, sin = lag_rotation(NW, NF, LAGS)
    scale = 1.0 / (NWIN * NF)
    cos = cos * scale
    sin = sin * scale
    rot_real = (
        own_real[:, :, None, :] * cos.T[None, None] - own_imag[:, :, None, :] * sin.T[None, None]
    )
    rot_imag = (
        own_real[:, :, None, :] * sin.T[None, None] + own_imag[:, :, None, :] * cos.T[None, None]
    )
    rotated = jnp.concatenate([rot_real, rot_imag], axis=-1).astype(jnp.bfloat16)
    result = jnp.einsum("wilk,wjk->ilj", rotated, others, preferred_element_type=jnp.float32)
    return result.astype(jnp.bfloat16)


def solution(mesh):
    placed = (P(("groups", "chan"), None), P(("groups", "chan")))
    return jax.shard_map(
        shards,
        mesh=mesh,
        in_specs=placed,
        out_specs=P(("groups", "chan"), None, None),
        check_vma=False,
    )
```

profile of v0, /device:TPU:0, one launch (start us, length us, event | category | flops | bytes accessed | tf_op | source)
XLA Modules:
  0.0 129.0 jit_solution(4269690971907902461)
XLA Ops:
  6.5 0.0 all-gather.2.cloned.1.call-start
  6.5 1.3 convert_reduce_fusion
  7.8 0.7 convert_element_type.48
  8.5 1.1 multiply_reduce_fusion
  9.6 36.6 %all-reduce = (f32[1152]{0:T(1024)S(1)}, f32[]{:T(128)}) all-reduce(f32[1152]{0:T(1024)S(1)} %multiply_reduce_fusion, f32[]{:T(128)} %convert_reduce_fusion), channel_id=1, replica_groups=mesh['groups'=2,'chan'=16] {'chan'}, use_global_device_ids=true, to_apply=%region_1.0 | all-reduce | flops 1153 | bytes 9224 | tf_op jit(solution)/shard_map/psum | solution.py:36
  46.9 1.1 subtract_multiply_fusion
  48.0 0.1 copy.10
  48.1 0.1 copy.11
  48.2 0.5 cosine_multiply_fusion
  48.7 0.6 convolution_bitcast_fusion
  49.3 0.1 fusion.25
  49.5 0.2 divide_convert_fusion.1
  49.6 0.8 pad_maximum_fusion
  50.4 0.0 all-gather.2.cloned.1.call-update
  50.5 0.2 copy.7
  50.6 0.2 copy.8
  50.8 0.2 cosine_multiply_fusion.1
  51.0 7.5 %subtract_convert_fusion = (bf16[8,64,64,128]{3,2,0,1:T(8,128)(2,1)}, bf16[8,64,64,128]{3,2,0,1:T(8,128)(2,1)}) fusion(f32[64,128]{1,0:T(8,128)S(1)} %get-tuple-element.18, f32[8,64,128]{2,0,1:T(8,128)S(1)} %copy.8, f32[64,128]{1,0:T(8,128)S(1)} %get-tuple-element.17, f32[8,64,128]{2,0,1:T(8,128)S(1)} %copy.7), kind=kLoop, calls=%fused_computation.6 | loop fusion | flops 33554432 | bytes 17367040 | tf_op jit(solution)/shard_map/convert
  58.5 39.7 %all-gather.2.cloned.1.call-done = bf16[8,1024,256]{2,1,0:T(8,128)(2,1)} async-done(((bf16[8,64,256]{2,1,0:T(8,128)(2,1)}), bf16[8,1024,256]{2,1,0:T(8,128)(2,1)}) %all-gather.2.cloned.1.call-update) | async-done | bytes 4194320 | tf_op jit(solution)/shard_map/all_gather | solution.py:55
  98.2 24.0 %bitcast_convert_fusion = bf16[64,64,1024]{2,1,0:T(8,128)(2,1)} fusion(bf16[8,64,64,128]{3,2,0,1:T(8,128)(2,1)} %get-tuple-element.8, bf16[8,64,64,128]{3,2,0,1:T(8,128)(2,1)} %get-tuple-element.7, bf16[8,1024,256]{2,1,0:T(8,128)(2,1)} %all-gather.2.cloned.1.call-done), kind=kOutput, calls=%fused_computation.4 | convolution fusion | flops 17217617920 | bytes 29360128 | tf_op jit(solution)/shard_map/wilk,wjk->ilj/dot_general | solution.py:69
  (8 shorter events, 0.2 us)
Async XLA Ops:
  6.5 91.7 %all-gather.2.cloned.1.call-start = ((), (), s32[]{:S(2)}) async-start(), calls=%async_computation | async-start | bytes 4456448 | tf_op jit(solution)/shard_map/all_gather | solution.py:55
Sparse Core Ops, SparseCore 0:
  50.5 47.6 all-gather.1
where the time goes:
time: 129 us
  waiting for transfers between devices  39.7 us (31%)
  blocking collectives  36.6 us (28%)
  matrix products  24.6 us (19%)
  between operations  14.1 us (11%)
  other arithmetic  13.4 us (10%)
    all_gather x1, waiting for transfers between devices, shards(): others = lax.all_gather(whitened, 'chan', axis=1, tiled=True)  39.7 us
    psum x1, blocking collectives, whiten(): lax.psum((jnp.sum(traces * good[:, None], axis=0), jnp.sum(good)), 'chan')  36.6 us
    dot_general x1, matrix products, shards(): jnp.einsum('wilk,wjk->ilj', rotated, others, preferred_element_type=jnp.f...  24 us
    another operation x2, other arithmetic  7.65 us
  transfers between devices with their start and end apart: 1, of which 1 were waited for; matrix products, arithmetic and copies ran while one was open for 6% of the time, Pallas kernels for 0%

commit v1 on v0

--- a/solution.py
+++ b/solution.py
@@ -52,7 +52,6 @@
 
 def shards(traces, good_mask):
     whitened = whiten(traces, good_mask)
-    others = lax.all_gather(whitened, "chan", axis=1, tiled=True)
     own = whitened.astype(jnp.float32)
     own_real, own_imag = (own[..., :NF], own[..., NF:])
     cos, sin = lag_rotation(NW, NF, LAGS)
@@ -66,7 +65,21 @@
         own_real[:, :, None, :] * sin.T[None, None] + own_imag[:, :, None, :] * cos.T[None, None]
     )
     rotated = jnp.concatenate([rot_real, rot_imag], axis=-1).astype(jnp.bfloat16)
-    result = jnp.einsum("wilk,wjk->ilj", rotated, others, preferred_element_type=jnp.float32)
+    ways, here, step = (lax.axis_size("chan"), lax.axis_index("chan"), whitened.shape[1])
+    earlier, later = ([], [])
+    going_up = going_down = whitened
+    for far in range(ways // 2 + 1):
+        earlier.append(
+            jnp.einsum("wilk,wjk->ilj", rotated, going_up, preferred_element_type=jnp.float32)
+        )
+        if 0 < far < ways - ways // 2:
+            later.append(
+                jnp.einsum("wilk,wjk->ilj", rotated, going_down, preferred_element_type=jnp.float32)
+            )
+        going_up = lax.ppermute(going_up, "chan", [(d, (d + 1) % ways) for d in range(ways)])
+        going_down = lax.ppermute(going_down, "chan", [(d, (d - 1) % ways) for d in range(ways)])
+    line = jnp.concatenate([*earlier[::-1], *later], axis=2)
+    result = jnp.roll(line, (here - ways // 2) * earlier[0].shape[2], axis=2)
     return result.astype(jnp.bfloat16)
 
 

time: 129 us -> 235 us (1.82); the launches traced: 129 us -> 231 us
  matrix products: 24.6 us -> 99.2 us
  local copies, waits for them, and re-layouts: 0.55 us -> 52.1 us
  waiting for transfers between devices: 39.7 us -> 5.6 us
  starting transfers between devices: 0.01 us -> 26.8 us
  between operations: 14.1 us -> 0.87 us
  other arithmetic: 13.4 us -> 9.64 us
    dot_general x1 -> x16, matrix products: 24 us -> 98.6 us  [the longest x9 55.3 us: shards(): jnp.einsum('wilk,wjk->ilj', rotated, going_up, preferred_element_type=jnp...]
    all_gather x1 -> x0, waiting for transfers between devices: 39.7 us -> none  [shards(): others = lax.all_gather(whitened, 'chan', axis=1, tiled=True)]
    concatenate x0 -> x1, local copies, waits for them, and re-layouts: none -> 39 us  [shards(): result = jnp.roll(line, (here - ways // 2) * earlier[0].shape[2], axis=2)]
    ppermute x0 -> x15, starting transfers between devices: none -> 26.8 us  [the longest x7 26.3 us: shards(): lax.ppermute(going_down, 'chan', [(d, (d - 1) % ways) for d in range(ways)])]
    convert_element_type x0 -> x1, local copies, waits for them, and re-layouts: none -> 12.6 us  [shards(): return result.astype(jnp.bfloat16)]
    ppermute x0 -> x15, waiting for transfers between devices: none -> 5.6 us  [the longest x8 5.58 us: shards(): lax.ppermute(going_up, 'chan', [(d, (d + 1) % ways) for d in range(ways)])]
    another operation x2, other arithmetic: 7.65 us -> 4.59 us
  transfers between devices with their start and end apart: 1 -> 15, of which waited for: 1 -> 2; matrix products, arithmetic and copies ran while one was open for 6% -> 42% of each run, Pallas kernels for 0% -> 0%
where the time goes in v1:
time: 235 us; the launch traced here: 231 us
  matrix products  99.2 us (42%)
  local copies, waits for them, and re-layouts  52.1 us (22%)
  blocking collectives  36.6 us (16%)
  starting transfers between devices  26.8 us (11%)
  other arithmetic  9.64 us (4%)
  waiting for transfers between devices  5.6 us (2%)
    dot_general x9, matrix products, shards(): jnp.einsum('wilk,wjk->ilj', rotated, going_up, preferred_element_type=jnp...  55.3 us
    dot_general x7, matrix products, shards(): jnp.einsum('wilk,wjk->ilj', rotated, going_down, preferred_element_type=j...  43.4 us
    concatenate x1, local copies, waits for them, and re-layouts, shards(): result = jnp.roll(line, (here - ways // 2) * earlier[0].shape[2], axis=2)  39 us
    psum x1, blocking collectives, whiten(): lax.psum((jnp.sum(traces * good[:, None], axis=0), jnp.sum(good)), 'chan')  36.6 us
    ppermute x7, starting transfers between devices, shards(): lax.ppermute(going_down, 'chan', [(d, (d - 1) % ways) for d in range(ways)])  26.3 us
    convert_element_type x1, local copies, waits for them, and re-layouts, shards(): return result.astype(jnp.bfloat16)  12.6 us
    ppermute x8, waiting for transfers between devices, shards(): lax.ppermute(going_up, 'chan', [(d, (d + 1) % ways) for d in range(ways)])  5.58 us
  transfers between devices with their start and end apart: 15, of which 2 were waited for; matrix products, arithmetic and copies ran while one was open for 42% of the time, Pallas kernels for 0%

profile of v1, /device:TPU:0, one launch (start us, length us, event | category | flops | bytes accessed | tf_op | source)
XLA Modules:
  0.0 230.9 jit_solution(13232363081643385098)
XLA Ops:
  0.0 0.7 convert_element_type.48
  0.7 1.3 convert_reduce_fusion
  2.0 1.1 multiply_reduce_fusion
  3.0 36.6 %all-reduce = (f32[1152]{0:T(1024)S(1)}, f32[]{:T(128)}) all-reduce(f32[1152]{0:T(1024)S(1)} %multiply_reduce_fusion, f32[]{:T(128)} %convert_reduce_fusion), channel_id=1, replica_groups=mesh['groups'=2,'chan'=16] {'chan'}, use_global_device_ids=true, to_apply=%region_1.0 | all-reduce | flops 1153 | bytes 9224 | tf_op jit(solution)/shard_map/psum | solution.py:36
  40.3 1.1 subtract_multiply_fusion
  44.3 4.4 %subtract_convert_fusion = (bf16[8,64,64,128]{3,2,0,1:T(8,128)(2,1)S(1)}, bf16[8,64,64,128]{3,2,0,1:T(8,128)(2,1)S(1)}) fusion(f32[64,128]{1,0:T(8,128)S(1)} %get-tuple-element.18, f32[8,64,128]{2,0,1:T(8,128)S(1)} %copy.8, f32[64,128]{1,0:T(8,128)S(1)} %get-tuple-element.17, f32[8,64,128]{2,0,1:T(8,128)S(1)} %copy.7), kind=kLoop, calls=%fused_computation.3 | loop fusion | flops 33554432 | bytes 17367040 | tf_op jit(solution)/shard_map/convert
  48.8 6.3 %convolution_bitcast_fusion.7 = bf16[64,64,64]{2,1,0:T(8,128)(2,1)} fusion(bf16[8,64,128]{2,1,0:T(8,128)(2,1)S(1)} %get-tuple-element.10, bf16[8,64,128]{2,1,0:T(8,128)(2,1)S(1)} %get-tuple-element.9, bf16[8,64,64,128]{3,2,0,1:T(8,128)(2,1)S(1)} %get-tuple-element.8, bf16[8,64,64,128]{3,2,0,1:T(8,128)(2,1)S(1)} %get-tuple-element.7), kind=kOutput, calls=%fused_computation.11 | convolution fusion | flops 1107820544 | bytes 17563648 | tf_op jit(solution)/shard_map/wilk,wjk->ilj/dot_general | solution.py:73
  55.1 4.0 %collective-permute-start.9 = (bf16[8,64,256]{2,1,0:T(8,128)(2,1)S(1)}, bf16[8,64,256]{2,1,0:T(8,128)(2,1)S(1)}, u32[]{:S(2)}, u32[]{:S(2)}) collective-permute-start(bf16[8,64,256]{2,1,0:T(8,128)(2,1)S(1)} %collective-permute-done.8), channel_id=1, source_target_pairs={{0,15},{1,0},{2,1},{3,2},{4,3},{5,4},{6,5},{7,6},{8,7},{9,8},{10,9... | collective-permute-start | bytes 786440 | tf_op jit(solution)/shard_map/ppermute | solution.py:80
  59.1 9.2 %convolution_bitcast_fusion.6 = bf16[64,64,64]{2,1,0:T(8,128)(2,1)} fusion(bf16[8,64,256]{2,1,0:T(8,128)(2,1)S(1)} %collective-permute-done.8, bf16[8,64,64,128]{3,2,0,1:T(8,128)(2,1)} %copy-done.1, bf16[8,64,64,128]{3,2,0,1:T(8,128)(2,1)} %copy-done), kind=kOutput, calls=%fused_computation.10 | convolution fusion | flops 1107296256 | bytes 17563648 | tf_op jit(solution)/shard_map/wilk,wjk->ilj/dot_general | solution.py:77
  68.4 9.2 %convolution_bitcast_fusion.8 = bf16[64,64,64]{2,1,0:T(8,128)(2,1)} fusion(bf16[8,64,256]{2,1,0:T(8,128)(2,1)S(1)} %collective-permute-done, bf16[8,64,64,128]{3,2,0,1:T(8,128)(2,1)} %copy-done.1, bf16[8,64,64,128]{3,2,0,1:T(8,128)(2,1)} %copy-done), kind=kOutput, calls=%fused_computation.12 | convolution fusion | flops 1107296256 | bytes 17563648 | tf_op jit(solution)/shard_map/wilk,wjk->ilj/dot_general | solution.py:73
  77.6 4.4 %collective-permute-start.10 = (bf16[8,64,256]{2,1,0:T(8,128)(2,1)S(1)}, bf16[8,64,256]{2,1,0:T(8,128)(2,1)S(1)}, u32[]{:S(2)}, u32[]{:S(2)}) collective-permute-start(bf16[8,64,256]{2,1,0:T(8,128)(2,1)S(1)} %collective-permute-done.9), channel_id=1, source_target_pairs={{0,15},{1,0},{2,1},{3,2},{4,3},{5,4},{6,5},{7,6},{8,7},{9,8},{10,9... | collective-permute-start | bytes 786440 | tf_op jit(solution)/shard_map/ppermute | solution.py:80
  82.1 5.7 %convolution_bitcast_fusion.5 = bf16[64,64,64]{2,1,0:T(8,128)(2,1)} fusion(bf16[8,64,256]{2,1,0:T(8,128)(2,1)S(1)} %collective-permute-done.9, bf16[8,64,64,128]{3,2,0,1:T(8,128)(2,1)S(1)} %bitcast.104, bf16[8,64,64,128]{3,2,0,1:T(8,128)(2,1)S(1)} %bitcast.102), kind=kOutput, calls=%fused_computation.9 | convolution fusion | flops 1107296256 | bytes 17563648 | tf_op jit(solution)/shard_map/wilk,wjk->ilj/dot_general | solution.py:77
  87.8 5.7 %convolution_bitcast_fusion.9 = bf16[64,64,64]{2,1,0:T(8,128)(2,1)} fusion(bf16[8,64,256]{2,1,0:T(8,128)(2,1)S(1)} %collective-permute-done.1, bf16[8,64,64,128]{3,2,0,1:T(8,128)(2,1)S(1)} %bitcast.104, bf16[8,64,64,128]{3,2,0,1:T(8,128)(2,1)S(1)} %bitcast.102), kind=kOutput, calls=%fused_computation.13 | convolution fusion | flops 1107296256 | bytes 17563648 | tf_op jit(solution)/shard_map/wilk,wjk->ilj/dot_general | solution.py:73
  93.5 4.4 %collective-permute-start.11 = (bf16[8,64,256]{2,1,0:T(8,128)(2,1)S(1)}, bf16[8,64,256]{2,1,0:T(8,128)(2,1)S(1)}, u32[]{:S(2)}, u32[]{:S(2)}) collective-permute-start(bf16[8,64,256]{2,1,0:T(8,128)(2,1)S(1)} %collective-permute-done.10), channel_id=1, source_target_pairs={{0,15},{1,0},{2,1},{3,2},{4,3},{5,4},{6,5},{7,6},{8,7},{9,8},{10,9... | collective-permute-start | bytes 786440 | tf_op jit(solution)/shard_map/ppermute | solution.py:80
  97.9 5.7 %convolution_bitcast_fusion.4 = bf16[64,64,64]{2,1,0:T(8,128)(2,1)} fusion(bf16[8,64,256]{2,1,0:T(8,128)(2,1)S(1)} %collective-permute-done.10, bf16[8,64,64,128]{3,2,0,1:T(8,128)(2,1)S(1)} %bitcast.104, bf16[8,64,64,128]{3,2,0,1:T(8,128)(2,1)S(1)} %bitcast.102), kind=kOutput, calls=%fused_computation.8 | convolution fusion | flops 1107296256 | bytes 17563648 | tf_op jit(solution)/shard_map/wilk,wjk->ilj/dot_general | solution.py:77
  103.6 5.7 %convolution_bitcast_fusion.10 = bf16[64,64,64]{2,1,0:T(8,128)(2,1)} fusion(bf16[8,64,256]{2,1,0:T(8,128)(2,1)S(1)} %collective-permute-done.2, bf16[8,64,64,128]{3,2,0,1:T(8,128)(2,1)S(1)} %bitcast.104, bf16[8,64,64,128]{3,2,0,1:T(8,128)(2,1)S(1)} %bitcast.102), kind=kOutput, calls=%fused_computation.14 | convolution fusion | flops 1107296256 | bytes 17563648 | tf_op jit(solution)/shard_map/wilk,wjk->ilj/dot_general | solution.py:73
  109.3 4.4 %collective-permute-start.12 = (bf16[8,64,256]{2,1,0:T(8,128)(2,1)S(1)}, bf16[8,64,256]{2,1,0:T(8,128)(2,1)S(1)}, u32[]{:S(2)}, u32[]{:S(2)}) collective-permute-start(bf16[8,64,256]{2,1,0:T(8,128)(2,1)S(1)} %collective-permute-done.11), channel_id=1, source_target_pairs={{0,15},{1,0},{2,1},{3,2},{4,3},{5,4},{6,5},{7,6},{8,7},{9,8},{10,9... | collective-permute-start | bytes 786440 | tf_op jit(solution)/shard_map/ppermute | solution.py:80
  113.7 5.7 %convolution_bitcast_fusion.3 = bf16[64,64,64]{2,1,0:T(8,128)(2,1)} fusion(bf16[8,64,256]{2,1,0:T(8,128)(2,1)S(1)} %collective-permute-done.11, bf16[8,64,64,128]{3,2,0,1:T(8,128)(2,1)S(1)} %bitcast.104, bf16[8,64,64,128]{3,2,0,1:T(8,128)(2,1)S(1)} %bitcast.102), kind=kOutput, calls=%fused_computation.7 | convolution fusion | flops 1107296256 | bytes 17563648 | tf_op jit(solution)/shard_map/wilk,wjk->ilj/dot_general | solution.py:77
  119.4 5.7 %convolution_bitcast_fusion.11 = bf16[64,64,64]{2,1,0:T(8,128)(2,1)} fusion(bf16[8,64,256]{2,1,0:T(8,128)(2,1)S(1)} %collective-permute-done.3, bf16[8,64,64,128]{3,2,0,1:T(8,128)(2,1)S(1)} %bitcast.104, bf16[8,64,64,128]{3,2,0,1:T(8,128)(2,1)S(1)} %bitcast.102), kind=kOutput, calls=%fused_computation.15 | convolution fusion | flops 1107296256 | bytes 17563648 | tf_op jit(solution)/shard_map/wilk,wjk->ilj/dot_general | solution.py:73
  125.1 4.4 %collective-permute-start.13 = (bf16[8,64,256]{2,1,0:T(8,128)(2,1)S(1)}, bf16[8,64,256]{2,1,0:T(8,128)(2,1)S(1)}, u32[]{:S(2)}, u32[]{:S(2)}) collective-permute-start(bf16[8,64,256]{2,1,0:T(8,128)(2,1)S(1)} %collective-permute-done.12), channel_id=1, source_target_pairs={{0,15},{1,0},{2,1},{3,2},{4,3},{5,4},{6,5},{7,6},{8,7},{9,8},{10,9... | collective-permute-start | bytes 786440 | tf_op jit(solution)/shard_map/ppermute | solution.py:80
  129.6 5.7 %convolution_bitcast_fusion.2 = bf16[64,64,64]{2,1,0:T(8,128)(2,1)} fusion(bf16[8,64,256]{2,1,0:T(8,128)(2,1)S(1)} %collective-permute-done.12, bf16[8,64,64,128]{3,2,0,1:T(8,128)(2,1)S(1)} %bitcast.104, bf16[8,64,64,128]{3,2,0,1:T(8,128)(2,1)S(1)} %bitcast.102), kind=kOutput, calls=%fused_computation.6 | convolution fusion | flops 1107296256 | bytes 17563648 | tf_op jit(solution)/shard_map/wilk,wjk->ilj/dot_general | solution.py:77
  135.2 5.7 %convolution_bitcast_fusion.12 = bf16[64,64,64]{2,1,0:T(8,128)(2,1)} fusion(bf16[8,64,256]{2,1,0:T(8,128)(2,1)S(1)} %collective-permute-done.4, bf16[8,64,64,128]{3,2,0,1:T(8,128)(2,1)S(1)} %bitcast.104, bf16[8,64,64,128]{3,2,0,1:T(8,128)(2,1)S(1)} %bitcast.102), kind=kOutput, calls=%fused_computation.16 | convolution fusion | flops 1107296256 | bytes 17563648 | tf_op jit(solution)/shard_map/wilk,wjk->ilj/dot_general | solution.py:73
  140.9 4.4 %collective-permute-start.14 = (bf16[8,64,256]{2,1,0:T(8,128)(2,1)S(1)}, bf16[8,64,256]{2,1,0:T(8,128)(2,1)S(1)}, u32[]{:S(2)}, u32[]{:S(2)}) collective-permute-start(bf16[8,64,256]{2,1,0:T(8,128)(2,1)S(1)} %collective-permute-done.13), channel_id=1, source_target_pairs={{0,15},{1,0},{2,1},{3,2},{4,3},{5,4},{6,5},{7,6},{8,7},{9,8},{10,9... | collective-permute-start | bytes 786440 | tf_op jit(solution)/shard_map/ppermute | solution.py:80
  145.4 5.7 %convolution_bitcast_fusion.1 = bf16[64,64,64]{2,1,0:T(8,128)(2,1)} fusion(bf16[8,64,256]{2,1,0:T(8,128)(2,1)S(1)} %collective-permute-done.13, bf16[8,64,64,128]{3,2,0,1:T(8,128)(2,1)S(1)} %bitcast.104, bf16[8,64,64,128]{3,2,0,1:T(8,128)(2,1)S(1)} %bitcast.102), kind=kOutput, calls=%fused_computation.5 | convolution fusion | flops 1107296256 | bytes 17563648 | tf_op jit(solution)/shard_map/wilk,wjk->ilj/dot_general | solution.py:77
  151.0 5.7 %convolution_bitcast_fusion.13 = bf16[64,64,64]{2,1,0:T(8,128)(2,1)} fusion(bf16[8,64,256]{2,1,0:T(8,128)(2,1)S(1)} %collective-permute-done.5, bf16[8,64,64,128]{3,2,0,1:T(8,128)(2,1)S(1)} %bitcast.104, bf16[8,64,64,128]{3,2,0,1:T(8,128)(2,1)S(1)} %bitcast.102), kind=kOutput, calls=%fused_computation.17 | convolution fusion | flops 1107296256 | bytes 17563648 | tf_op jit(solution)/shard_map/wilk,wjk->ilj/dot_general | solution.py:73
  156.8 2.8 %collective-permute-done.6 = bf16[8,64,256]{2,1,0:T(8,128)(2,1)S(1)} collective-permute-done((bf16[8,64,256]{2,1,0:T(8,128)(2,1)S(1)}, bf16[8,64,256]{2,1,0:T(8,128)(2,1)S(1)}, u32[]{:S(2)}, u32[]{:S(2)}) %collective-permute-start.6) | collective-permute-done | bytes 262176 | tf_op jit(solution)/shard_map/ppermute | solution.py:79
  159.5 5.7 %convolution_bitcast_fusion.14 = bf16[64,64,64]{2,1,0:T(8,128)(2,1)} fusion(bf16[8,64,256]{2,1,0:T(8,128)(2,1)S(1)} %collective-permute-done.6, bf16[8,64,64,128]{3,2,0,1:T(8,128)(2,1)S(1)} %bitcast.104, bf16[8,64,64,128]{3,2,0,1:T(8,128)(2,1)S(1)} %bitcast.102), kind=kOutput, calls=%fused_computation.18 | convolution fusion | flops 1107296256 | bytes 17563648 | tf_op jit(solution)/shard_map/wilk,wjk->ilj/dot_general | solution.py:73
  165.2 5.7 %convolution_bitcast_fusion = bf16[64,64,64]{2,1,0:T(8,128)(2,1)} fusion(bf16[8,64,256]{2,1,0:T(8,128)(2,1)S(1)} %collective-permute-done.14, bf16[8,64,64,128]{3,2,0,1:T(8,128)(2,1)S(1)} %bitcast.104, bf16[8,64,64,128]{3,2,0,1:T(8,128)(2,1)S(1)} %bitcast.102), kind=kOutput, calls=%fused_computation.4 | convolution fusion | flops 1107296256 | bytes 17563648 | tf_op jit(solution)/shard_map/wilk,wjk->ilj/dot_general | solution.py:77
  170.9 2.8 %collective-permute-done.7 = bf16[8,64,256]{2,1,0:T(8,128)(2,1)S(1)} collective-permute-done((bf16[8,64,256]{2,1,0:T(8,128)(2,1)S(1)}, bf16[8,64,256]{2,1,0:T(8,128)(2,1)S(1)}, u32[]{:S(2)}, u32[]{:S(2)}) %collective-permute-start.7) | collective-permute-done | bytes 262176 | tf_op jit(solution)/shard_map/ppermute | solution.py:79
  173.7 5.7 %convolution_bitcast_fusion.15 = bf16[64,64,64]{2,1,0:T(8,128)(2,1)} fusion(bf16[8,64,256]{2,1,0:T(8,128)(2,1)S(1)} %collective-permute-done.7, bf16[8,64,64,128]{3,2,0,1:T(8,128)(2,1)S(1)} %bitcast.104, bf16[8,64,64,128]{3,2,0,1:T(8,128)(2,1)S(1)} %bitcast.102), kind=kOutput, calls=%fused_computation.19 | convolution fusion | flops 1107296256 | bytes 17563648 | tf_op jit(solution)/shard_map/wilk,wjk->ilj/dot_general | solution.py:73
  179.4 39.0 %concatenate.24 = bf16[64,64,2048]{2,1,0:T(8,128)(2,1)} concatenate(bf16[64,64,64]{2,1,0:T(8,128)(2,1)} %convolution_bitcast_fusion.15, bf16[64,64,64]{2,1,0:T(8,128)(2,1)} %convolution_bitcast_fusion.14, bf16[64,64,64]{2,1,0:T(8,128)(2,1)} %convolution_bitcast_fusion.13, bf16[64,64,64]{2,1,0:T(8,128)(2,1)} %convolution_bitcast_fusion.12, ...), dimensions={2} | concatenate | bytes 33554432 | tf_op jit(solution)/shard_map/jit(_roll_dynamic)/concatenate | solution.py:82
  218.3 12.6 %dynamic-slice_convert_fusion = bf16[64,64,1024]{2,1,0:T(8,128)(2,1)} fusion(bf16[64,64,2048]{2,1,0:T(8,128)(2,1)} %concatenate.24, s32[]{:T(128)S(6)} %select_n.45), kind=kLoop, calls=%fused_computation.1 | loop fusion | bytes 16777220 | tf_op jit(solution)/shard_map/convert_element_type | solution.py:83
  (60 shorter events, 3.0 us)
Async XLA Ops:
  43.2 11.9 %collective-permute-start.8 = (bf16[8,64,256]{2,1,0:T(8,128)(2,1)S(1)}, bf16[8,64,256]{2,1,0:T(8,128)(2,1)S(1)}, u32[]{:S(2)}, u32[]{:S(2)}) collective-permute-start(bf16[8,64,256]{2,1,0:T(8,128)(2,1)S(1)} %get-tuple-element.16), channel_id=1, source_target_pairs={{0,15},{1,0},{2,1},{3,2},{4,3},{5,4},{6,5},{7,6},{8,7},{9,8},{10,9... | collective-permute-start | bytes 786440 | tf_op jit(solution)/shard_map/ppermute | solution.py:80
  43.2 25.1 %collective-permute-start = (bf16[8,64,256]{2,1,0:T(8,128)(2,1)S(1)}, bf16[8,64,256]{2,1,0:T(8,128)(2,1)S(1)}, u32[]{:S(2)}, u32[]{:S(2)}) collective-permute-start(bf16[8,64,256]{2,1,0:T(8,128)(2,1)S(1)} %get-tuple-element.16), channel_id=1, source_target_pairs={{0,1},{1,2},{2,3},{3,4},{4,5},{5,6},{6,7},{7,8},{8,9},{9,10},{10,1... | collective-permute-start | bytes 786440 | tf_op jit(solution)/shard_map/ppermute | solution.py:79
  48.8 6.3 %copy-start = (bf16[8,64,64,128]{3,2,0,1:T(8,128)(2,1)}, bf16[8,64,64,128]{3,2,0,1:T(8,128)(2,1)S(1)}, u32[]{:S(2)}) copy-start(bf16[8,64,64,128]{3,2,0,1:T(8,128)(2,1)S(1)} %get-tuple-element.7) | copy-start | bytes 25165828
  48.8 6.3 %copy-start.1 = (bf16[8,64,64,128]{3,2,0,1:T(8,128)(2,1)}, bf16[8,64,64,128]{3,2,0,1:T(8,128)(2,1)S(1)}, u32[]{:S(2)}) copy-start(bf16[8,64,64,128]{3,2,0,1:T(8,128)(2,1)S(1)} %get-tuple-element.8) | copy-start | bytes 25165828
  55.1 22.5 %collective-permute-start.9 = (bf16[8,64,256]{2,1,0:T(8,128)(2,1)S(1)}, bf16[8,64,256]{2,1,0:T(8,128)(2,1)S(1)}, u32[]{:S(2)}, u32[]{:S(2)}) collective-permute-start(bf16[8,64,256]{2,1,0:T(8,128)(2,1)S(1)} %collective-permute-done.8), channel_id=1, source_target_pairs={{0,15},{1,0},{2,1},{3,2},{4,3},{5,4},{6,5},{7,6},{8,7},{9,8},{10,9... | collective-permute-start | bytes 786440 | tf_op jit(solution)/shard_map/ppermute | solution.py:80
  59.1 22.9 %slice-start = ((s8[8388608]{0:T(1024)(128)(4,1)}), s8[4194304]{0:T(1024)(128)(4,1)S(1)}, s32[]{:S(2)}) async-start(s8[8388608]{0:T(1024)(128)(4,1)} %bitcast.101), calls=%async_computation | async-start | bytes 8388608
  59.1 22.9 %slice-start.2 = ((s8[8388608]{0:T(1024)(128)(4,1)}), s8[4194304]{0:T(1024)(128)(4,1)S(1)}, s32[]{:S(2)}) async-start(s8[8388608]{0:T(1024)(128)(4,1)} %bitcast.103), calls=%async_computation.2 | async-start | bytes 8388608
  68.3 13.7 %slice-start.1 = ((s8[8388608]{0:T(1024)(128)(4,1)}), s8[4194304]{0:T(1024)(128)(4,1)S(1)}, s32[]{:S(2)}) async-start(s8[8388608]{0:T(1024)(128)(4,1)} %bitcast.101), calls=%async_computation.1 | async-start | bytes 8388608
  68.4 13.7 %slice-start.3 = ((s8[8388608]{0:T(1024)(128)(4,1)}), s8[4194304]{0:T(1024)(128)(4,1)S(1)}, s32[]{:S(2)}) async-start(s8[8388608]{0:T(1024)(128)(4,1)} %bitcast.103), calls=%async_computation.3 | async-start | bytes 8388608
  77.6 10.2 %collective-permute-start.1 = (bf16[8,64,256]{2,1,0:T(8,128)(2,1)S(1)}, bf16[8,64,256]{2,1,0:T(8,128)(2,1)S(1)}, u32[]{:S(2)}, u32[]{:S(2)}) collective-permute-start(bf16[8,64,256]{2,1,0:T(8,128)(2,1)S(1)} %collective-permute-done), channel_id=1, source_target_pairs={{0,1},{1,2},{2,3},{3,4},{4,5},{5,6},{6,7},{7,8},{8,9},{9,10},{10,1... | collective-permute-start | bytes 786440 | tf_op jit(solution)/shard_map/ppermute | solution.py:79
  77.6 15.9 %collective-permute-start.10 = (bf16[8,64,256]{2,1,0:T(8,128)(2,1)S(1)}, bf16[8,64,256]{2,1,0:T(8,128)(2,1)S(1)}, u32[]{:S(2)}, u32[]{:S(2)}) collective-permute-start(bf16[8,64,256]{2,1,0:T(8,128)(2,1)S(1)} %collective-permute-done.9), channel_id=1, source_target_pairs={{0,15},{1,0},{2,1},{3,2},{4,3},{5,4},{6,5},{7,6},{8,7},{9,8},{10,9... | collective-permute-start | bytes 786440 | tf_op jit(solution)/shard_map/ppermute | solution.py:80
  93.5 10.2 %collective-permute-start.2 = (bf16[8,64,256]{2,1,0:T(8,128)(2,1)S(1)}, bf16[8,64,256]{2,1,0:T(8,128)(2,1)S(1)}, u32[]{:S(2)}, u32[]{:S(2)}) collective-permute-start(bf16[8,64,256]{2,1,0:T(8,128)(2,1)S(1)} %collective-permute-done.1), channel_id=1, source_target_pairs={{0,1},{1,2},{2,3},{3,4},{4,5},{5,6},{6,7},{7,8},{8,9},{9,10},{10,1... | collective-permute-start | bytes 786440 | tf_op jit(solution)/shard_map/ppermute | solution.py:79
  93.5 15.8 %collective-permute-start.11 = (bf16[8,64,256]{2,1,0:T(8,128)(2,1)S(1)}, bf16[8,64,256]{2,1,0:T(8,128)(2,1)S(1)}, u32[]{:S(2)}, u32[]{:S(2)}) collective-permute-start(bf16[8,64,256]{2,1,0:T(8,128)(2,1)S(1)} %collective-permute-done.10), channel_id=1, source_target_pairs={{0,15},{1,0},{2,1},{3,2},{4,3},{5,4},{6,5},{7,6},{8,7},{9,8},{10,9... | collective-permute-start | bytes 786440 | tf_op jit(solution)/shard_map/ppermute | solution.py:80
  109.3 10.1 %collective-permute-start.3 = (bf16[8,64,256]{2,1,0:T(8,128)(2,1)S(1)}, bf16[8,64,256]{2,1,0:T(8,128)(2,1)S(1)}, u32[]{:S(2)}, u32[]{:S(2)}) collective-permute-start(bf16[8,64,256]{2,1,0:T(8,128)(2,1)S(1)} %collective-permute-done.2), channel_id=1, source_target_pairs={{0,1},{1,2},{2,3},{3,4},{4,5},{5,6},{6,7},{7,8},{8,9},{9,10},{10,1... | collective-permute-start | bytes 786440 | tf_op jit(solution)/shard_map/ppermute | solution.py:79
  109.3 15.8 %collective-permute-start.12 = (bf16[8,64,256]{2,1,0:T(8,128)(2,1)S(1)}, bf16[8,64,256]{2,1,0:T(8,128)(2,1)S(1)}, u32[]{:S(2)}, u32[]{:S(2)}) collective-permute-start(bf16[8,64,256]{2,1,0:T(8,128)(2,1)S(1)} %collective-permute-done.11), channel_id=1, source_target_pairs={{0,15},{1,0},{2,1},{3,2},{4,3},{5,4},{6,5},{7,6},{8,7},{9,8},{10,9... | collective-permute-start | bytes 786440 | tf_op jit(solution)/shard_map/ppermute | solution.py:80
  125.1 10.1 %collective-permute-start.4 = (bf16[8,64,256]{2,1,0:T(8,128)(2,1)S(1)}, bf16[8,64,256]{2,1,0:T(8,128)(2,1)S(1)}, u32[]{:S(2)}, u32[]{:S(2)}) collective-permute-start(bf16[8,64,256]{2,1,0:T(8,128)(2,1)S(1)} %collective-permute-done.3), channel_id=1, source_target_pairs={{0,1},{1,2},{2,3},{3,4},{4,5},{5,6},{6,7},{7,8},{8,9},{9,10},{10,1... | collective-permute-start | bytes 786440 | tf_op jit(solution)/shard_map/ppermute | solution.py:79
  125.1 15.8 %collective-permute-start.13 = (bf16[8,64,256]{2,1,0:T(8,128)(2,1)S(1)}, bf16[8,64,256]{2,1,0:T(8,128)(2,1)S(1)}, u32[]{:S(2)}, u32[]{:S(2)}) collective-permute-start(bf16[8,64,256]{2,1,0:T(8,128)(2,1)S(1)} %collective-permute-done.12), channel_id=1, source_target_pairs={{0,15},{1,0},{2,1},{3,2},{4,3},{5,4},{6,5},{7,6},{8,7},{9,8},{10,9... | collective-permute-start | bytes 786440 | tf_op jit(solution)/shard_map/ppermute | solution.py:80
  140.9 10.1 %collective-permute-start.5 = (bf16[8,64,256]{2,1,0:T(8,128)(2,1)S(1)}, bf16[8,64,256]{2,1,0:T(8,128)(2,1)S(1)}, u32[]{:S(2)}, u32[]{:S(2)}) collective-permute-start(bf16[8,64,256]{2,1,0:T(8,128)(2,1)S(1)} %collective-permute-done.4), channel_id=1, source_target_pairs={{0,1},{1,2},{2,3},{3,4},{4,5},{5,6},{6,7},{7,8},{8,9},{9,10},{10,1... | collective-permute-start | bytes 786440 | tf_op jit(solution)/shard_map/ppermute | solution.py:79
  140.9 24.3 %collective-permute-start.14 = (bf16[8,64,256]{2,1,0:T(8,128)(2,1)S(1)}, bf16[8,64,256]{2,1,0:T(8,128)(2,1)S(1)}, u32[]{:S(2)}, u32[]{:S(2)}) collective-permute-start(bf16[8,64,256]{2,1,0:T(8,128)(2,1)S(1)} %collective-permute-done.13), channel_id=1, source_target_pairs={{0,15},{1,0},{2,1},{3,2},{4,3},{5,4},{6,5},{7,6},{8,7},{9,8},{10,9... | collective-permute-start | bytes 786440 | tf_op jit(solution)/shard_map/ppermute | solution.py:80
  151.0 8.5 %collective-permute-start.6 = (bf16[8,64,256]{2,1,0:T(8,128)(2,1)S(1)}, bf16[8,64,256]{2,1,0:T(8,128)(2,1)S(1)}, u32[]{:S(2)}, u32[]{:S(2)}) collective-permute-start(bf16[8,64,256]{2,1,0:T(8,128)(2,1)S(1)} %collective-permute-done.5), channel_id=1, source_target_pairs={{0,1},{1,2},{2,3},{3,4},{4,5},{5,6},{6,7},{7,8},{8,9},{9,10},{10,1... | collective-permute-start | bytes 786440 | tf_op jit(solution)/shard_map/ppermute | solution.py:79
  165.2 8.5 %collective-permute-start.7 = (bf16[8,64,256]{2,1,0:T(8,128)(2,1)S(1)}, bf16[8,64,256]{2,1,0:T(8,128)(2,1)S(1)}, u32[]{:S(2)}, u32[]{:S(2)}) collective-permute-start(bf16[8,64,256]{2,1,0:T(8,128)(2,1)S(1)} %collective-permute-done.6), channel_id=1, source_target_pairs={{0,1},{1,2},{2,3},{3,4},{4,5},{5,6},{6,7},{7,8},{8,9},{9,10},{10,1... | collective-permute-start | bytes 786440 | tf_op jit(solution)/shard_map/ppermute | solution.py:79
  170.9 8.4 %copy-start.2 = (bf16[64,64,64]{2,1,0:T(8,128)(2,1)S(1)}, bf16[64,64,64]{2,1,0:T(8,128)(2,1)}, u32[]{:S(2)}) copy-start(bf16[64,64,64]{2,1,0:T(8,128)(2,1)} %convolution_bitcast_fusion.7) | copy-start | bytes 1572868
  170.9 8.4 %copy-start.3 = (bf16[64,64,64]{2,1,0:T(8,128)(2,1)S(1)}, bf16[64,64,64]{2,1,0:T(8,128)(2,1)}, u32[]{:S(2)}) copy-start(bf16[64,64,64]{2,1,0:T(8,128)(2,1)} %convolution_bitcast_fusion.6) | copy-start | bytes 1572868
  170.9 8.4 %copy-start.4 = (bf16[64,64,64]{2,1,0:T(8,128)(2,1)S(1)}, bf16[64,64,64]{2,1,0:T(8,128)(2,1)}, u32[]{:S(2)}) copy-start(bf16[64,64,64]{2,1,0:T(8,128)(2,1)} %convolution_bitcast_fusion.8) | copy-start | bytes 1572868
